TPU v7x, 32 devices: a whole 2x2x4 slice. The times are simulated.
32 devices in a mesh: rep: 8 (over z, x), tile: 4 (over y, core).
Axes of the slice: x: 2, y: 2, z: 4, core: 2. Of those that a mesh axis runs over, the one named last changes fastest.
Arguments:
- features: bfloat16 [16, 48, 72, 1536], P('rep', 'tile'), may hold values from -6 to 6
- conv_out: bfloat16 [16, 48, 72, 256], P('rep', 'tile'), may hold values from -6 to 6
- conv_weight: bfloat16 [9, 1536, 256], replicated, may hold values from -0.0546875 to 0.0546875
- norm_gain_vector: float32 [256], replicated, may hold values from 0.5 to 1.5
- norm_shift_vector: float32 [256], replicated, may hold values from -3 to 3
- class_map: float32 [3, 256], replicated, may hold values from -3 to 3
- labels: int32 [16, 48, 72], P('rep', 'tile'), may hold values from 0 to 2
- class_weight: int32 [3], replicated, may hold values from 1 to 39
Outputs:
- grad_features: bfloat16 [16, 48, 72, 1536], P('rep', 'tile')
- grad_weight: float32 [1536, 9, 256], P(('rep', 'tile'))
- grad_gain: float32 [256], replicated
- grad_shift: float32 [256], replicated
- grad_class: float32 [3, 256], replicated
- loss: float32 [], replicated
All inputs are finite; a program needn't handle non-finite values.
Results may differ from a plain program's by a relative error of at most 0.0049.
Values may be sent and summed in bfloat16 or wider, within the bound.
No kernel may reach another device: no remote copies, remote signals or barrier semaphores. Data moves between devices by JAX's collectives and lax.ppermute only.
A program may use at most 256 MiB of HBM per device.

v0:
```python
import jax
import jax.numpy as jnp
from jax import lax
from jax.sharding import PartitionSpec as P

IMG_DEV = 2
H = 48
W = 72
RATE = 12


def padded(x, sides, width):
    for axis, dim in sides:
        size, length = (lax.axis_size(axis), x.shape[dim])
        up = [(i, (i + 1) % size) for i in range(size - 1)]
        down = [(j, i) for i, j in up]
        last = lax.slice_in_dim(x, length - width, length, axis=dim)
        first = lax.slice_in_dim(x, 0, width, axis=dim)
        before = lax.ppermute(last, axis, up)
        after = lax.ppermute(first, axis, down)
        x = jnp.concatenate([before, x, after], axis=dim)
    return x


def body(
    features,
    conv_out,
    conv_weight,
    norm_gain_vector,
    norm_shift_vector,
    class_map,
    labels,
    class_weight,
):
    highest = lax.Precision.HIGHEST
    images, tile_rows, columns, in_chans = features.shape
    out_chans = conv_out.shape[3]
    local_pix = images * tile_rows * columns
    per_replica_part = IMG_DEV * H * W
    all_pix = lax.axis_size("rep") * per_replica_part
    yvals = conv_out.astype(jnp.float32).reshape(local_pix, out_chans)
    column_sum = lax.psum(jnp.sum(yvals, 0), "tile")
    centre_offset = yvals - column_sum / per_replica_part
    variance = lax.psum(jnp.sum(centre_offset * centre_offset, 0), "tile") / per_replica_part
    inverse_deviation = lax.rsqrt(variance + 1e-05)
    normalized_input = centre_offset * inverse_deviation
    preactivation_values = norm_gain_vector * normalized_input + norm_shift_vector
    zvals = jnp.maximum(preactivation_values, 0.0)
    logits = jnp.dot(zvals, class_map.T, precision=highest)
    onehot = (
        labels.reshape(local_pix, 1) == jnp.arange(class_map.shape[0], dtype=jnp.int32)
    ).astype(jnp.float32)
    weights_pix = jnp.sum(onehot * class_weight.astype(jnp.float32), -1)
    top_val = jnp.max(logits, -1, keepdims=True)
    log_total = top_val[:, 0] + jnp.log(jnp.sum(jnp.exp(logits - top_val), -1))
    cross = log_total - jnp.sum(onehot * logits, -1)
    weight_total, loss_total = lax.psum(
        (jnp.sum(weights_pix), jnp.sum(weights_pix * cross)), ("rep", "tile")
    )
    mean_weight = weight_total / all_pix
    loss = loss_total / mean_weight / all_pix
    probs = jnp.exp(logits - log_total[:, None])
    grad_logit = (weights_pix / mean_weight)[:, None] * (probs - onehot)
    class_local_slice = jnp.dot(grad_logit.T, zvals, precision=highest)
    grad_z = jnp.dot(grad_logit, class_map, precision=highest)
    preactivation_gradient = jnp.where(preactivation_values > 0, grad_z, 0.0)
    first_gradient_sum, second_gradient_sum, class_tile = lax.psum(
        (
            jnp.sum(preactivation_gradient, 0),
            jnp.sum(preactivation_gradient * normalized_input, 0),
            class_local_slice,
        ),
        "tile",
    )
    grad_shift, grad_gain, grad_class = lax.psum(
        (first_gradient_sum, second_gradient_sum, class_tile), "rep"
    )
    normalized_output_gradient = (
        norm_gain_vector
        * inverse_deviation
        * (
            preactivation_gradient
            - first_gradient_sum / per_replica_part
            - normalized_input * second_gradient_sum / per_replica_part
        )
    ).astype(jnp.bfloat16)
    normalized_output_gradient = normalized_output_gradient.reshape(
        images, tile_rows, columns, out_chans
    )
    extended = padded(normalized_output_gradient, (("tile", 1),), RATE)
    extended = jnp.pad(extended, ((0, 0), (0, 0), (RATE, RATE), (0, 0)))
    shifted_list = []
    for tap_index in range(9):
        row_off = RATE - (tap_index // 3 - 1) * RATE
        col_off = RATE - (tap_index % 3 - 1) * RATE
        piece = extended[:, row_off : row_off + tile_rows, col_off : col_off + columns, :]
        shifted_list.append(piece.reshape(local_pix, out_chans))
    accum_grad = jnp.zeros((local_pix, in_chans), jnp.float32)
    for tap_index in range(9):
        accum_grad = accum_grad + lax.dot_general(
            shifted_list[tap_index],
            conv_weight[tap_index],
            (((1,), (1,)), ((), ())),
            preferred_element_type=jnp.float32,
        )
    grad_features = accum_grad.astype(jnp.bfloat16).reshape(images, tile_rows, columns, in_chans)
    flat_x = features.reshape(local_pix, in_chans)
    parts_list = [
        lax.dot_general(
            flat_x, shifted, (((0,), (0,)), ((), ())), preferred_element_type=jnp.float32
        )
        for shifted in shifted_list
    ]
    grad_weight = lax.psum_scatter(
        jnp.stack(parts_list, 1), ("rep", "tile"), scatter_dimension=0, tiled=True
    )
    return (grad_features, grad_weight, grad_gain, grad_shift, grad_class, loss)


def solution(mesh):
    in_specs = (
        P("rep", "tile", None, None),
        P("rep", "tile", None, None),
        P(),
        P(),
        P(),
        P(),
        P("rep", "tile", None),
        P(),
    )
    out_specs = (P("rep", "tile", None, None), P(("rep", "tile"), None, None), P(), P(), P(), P())
    return jax.shard_map(body, mesh=mesh, in_specs=in_specs, out_specs=out_specs, check_vma=False)
```

profile of v0, /device:TPU:0, one launch (start us, length us, event | category | flops | bytes accessed | tf_op | source)
XLA Modules:
  0.0 405.0 jit_solution(10787423601491690530)
XLA Ops:
  8.7 8.4 %psum.70 = f32[256]{0:T(256)S(1)} all-reduce(f32[256]{0:T(256)S(1)} %convert_reduce_fusion), channel_id=1, replica_groups=mesh['rep'=8,'tile'=4] {'tile'}, use_global_device_ids=true, to_apply=%region_1.0 | all-reduce | flops 256 | bytes 2048 | tf_op jit(solution)/shard_map/psum | solution.py:42
  18.5 5.8 %psum.71 = f32[256]{0:T(256)S(1)} all-reduce(f32[256]{0:T(256)S(1)} %multiply_reduce_fusion.1), channel_id=1, replica_groups=mesh['rep'=8,'tile'=4] {'tile'}, use_global_device_ids=true, to_apply=%region_3.0 | all-reduce | flops 256 | bytes 2048 | tf_op jit(solution)/shard_map/psum | solution.py:44
  31.5 39.9 %all-reduce.1 = (f32[]{:T(128)}, f32[]{:T(128)}) all-reduce(f32[]{:T(128)} %get-tuple-element.31, f32[]{:T(128)} %get-tuple-element.40), channel_id=1, replica_groups=mesh['rep'=8,'tile'=4] {'rep','tile'}, use_global_device_ids=true, to_apply=%region_6.0 | all-reduce | flops 2 | bytes 16 | tf_op jit(solution)/shard_map/psum | solution.py:57
  73.1 4.6 %fusion.61 = (f32[256]{0:T(256)S(1)}, f32[256]{0:T(256)S(1)}, f32[1728,256]{1,0:T(8,128)}) fusion(f32[256]{0:T(256)S(1)} %get-tuple-element.49, f32[256]{0:T(256)S(1)} %broadcast_multiply_fusion.1, bf16[2,12,72,256]{3,2,1,0:T(8,128)(2,1)} %param.9, f32[3,256]{1,0:T(4,128)S(1)} %copy-done, f32[1728,3]{0,1:T(4,128)S(1)} %get-tuple-element.51, ...), kind=kOutput, calls=%fused_computation.92 | convolution fusion | flops 20374336 | bytes 4474368 | tf_op jit(solution)/shard_map/dot_general | solution.py:65
  77.6 6.9 %all-reduce.3 = (f32[256]{0:T(256)S(1)}, f32[256]{0:T(256)S(1)}, f32[3,256]{1,0:T(4,128)S(1)}) all-reduce(f32[256]{0:T(256)S(1)} %get-tuple-element.25, f32[256]{0:T(256)S(1)} %get-tuple-element.24, f32[3,256]{1,0:T(4,128)S(1)} %fusion.16), channel_id=1, replica_groups=mesh['rep'=8,'tile'=4] {'tile'}, use_global_device_ids=true, to_apply=%region_12.13 | all-reduce | flops 1280 | bytes 10240 | tf_op jit(solution)/shard_map/psum | solution.py:67
  90.4 3.8 collective-permute-done.1
  96.1 2.8 fusion.14
  101.7 2.8 fusion.12
  104.4 2.8 fusion.11
  107.2 2.8 fusion.10
  110.0 2.8 fusion.9
  115.5 2.8 fusion.7
  121.0 19.0 %copy.18 = f32[1536,9,256]{2,1,0:T(8,128)} copy(f32[1536,9,256]{0,2,1:T(8,128)} %fusion.6) | data formatting | bytes 28311552 | tf_op jit(solution)/shard_map/stack | solution.py:115
  140.7 21.3 %all-reduce.2 = (f32[256]{0:T(256)}, f32[256]{0:T(256)}, f32[3,256]{1,0:T(4,128)}) all-reduce(f32[256]{0:T(256)S(1)} %get-tuple-element.37, f32[256]{0:T(256)S(1)} %get-tuple-element.38, f32[3,256]{1,0:T(4,128)S(1)} %get-tuple-element.39), channel_id=1, replica_groups=mesh['rep'=8,'tile'=4] {'rep'}, use_global_device_ids=true, to_apply=%region_14.15 | all-reduce | flops 1280 | bytes 10240 | tf_op jit(solution)/shard_map/psum | solution.py:75
  162.0 7.7 %fusion.33 = f32[1728,1536]{1,0:T(8,128)} fusion(bf16[1728,256]{1,0:T(8,128)(2,1)S(1)} %multiply_convert_fusion, bf16[9,1536,256]{2,1,0:T(8,128)(2,1)} %param.10), kind=kOutput, calls=%fused_computation.52 | convolution fusion | flops 1358954496 | bytes 12288000 | tf_op jit(solution)/shard_map/dot_general | solution.py:100
  170.3 8.2 %fusion.26 = f32[1728,1536]{1,0:T(8,128)} fusion(bf16[1728,256]{1,0:T(8,128)(2,1)S(1)} %bitcast.174, bf16[9,1536,256]{2,1,0:T(8,128)(2,1)} %param.10), kind=kOutput, calls=%fused_computation.45 | convolution fusion | flops 1358954496 | bytes 12288000 | tf_op jit(solution)/shard_map/dot_general | solution.py:100
  178.5 6.4 %fusion.29 = f32[1728,1536]{1,0:T(8,128)} fusion(bf16[1728,256]{1,0:T(8,128)(2,1)S(1)} %bitcast.173, bf16[9,1536,256]{2,1,0:T(8,128)(2,1)S(1)} %bitcast.167), kind=kOutput, calls=%fused_computation.48 | convolution fusion | flops 1358954496 | bytes 12288000 | tf_op jit(solution)/shard_map/dot_general | solution.py:100
  184.9 6.3 %fusion.31 = f32[1728,1536]{1,0:T(8,128)} fusion(bf16[1728,256]{1,0:T(8,128)(2,1)S(1)} %bitcast.172, bf16[9,1536,256]{2,1,0:T(8,128)(2,1)S(1)} %bitcast.167), kind=kOutput, calls=%fused_computation.50 | convolution fusion | flops 1358954496 | bytes 12288000 | tf_op jit(solution)/shard_map/dot_general | solution.py:100
  191.2 6.3 %fusion.35 = f32[1728,1536]{1,0:T(8,128)} fusion(bf16[1728,256]{1,0:T(8,128)(2,1)S(1)} %bitcast.171, bf16[9,1536,256]{2,1,0:T(8,128)(2,1)S(1)} %bitcast.167), kind=kOutput, calls=%fused_computation.54 | convolution fusion | flops 1358954496 | bytes 12288000 | tf_op jit(solution)/shard_map/dot_general | solution.py:100
  197.6 5.7 %fusion.37 = f32[1728,1536]{1,0:T(8,128)} fusion(bf16[1728,256]{1,0:T(8,128)(2,1)S(1)} %bitcast.170, bf16[9,1536,256]{2,1,0:T(8,128)(2,1)S(1)} %bitcast.167), kind=kOutput, calls=%fused_computation.56 | convolution fusion | flops 1358954496 | bytes 12288000 | tf_op jit(solution)/shard_map/dot_general | solution.py:100
  203.3 5.6 %fusion.41 = f32[1728,1536]{1,0:T(8,128)} fusion(bf16[1728,256]{1,0:T(8,128)(2,1)S(1)} %bitcast.169, bf16[9,1536,256]{2,1,0:T(8,128)(2,1)S(1)} %bitcast.167), kind=kOutput, calls=%fused_computation.60 | convolution fusion | flops 1358954496 | bytes 12288000 | tf_op jit(solution)/shard_map/dot_general | solution.py:100
  209.0 6.2 %fusion.39 = f32[1728,1536]{1,0:T(8,128)} fusion(bf16[1728,256]{1,0:T(8,128)(2,1)S(1)} %bitcast.164, bf16[9,1536,256]{2,1,0:T(8,128)(2,1)S(1)} %bitcast.167), kind=kOutput, calls=%fused_computation.58 | convolution fusion | flops 1358954496 | bytes 12288000 | tf_op jit(solution)/shard_map/dot_general | solution.py:100
  215.1 30.1 %add_convert_fusion = bf16[1728,1536]{1,0:T(8,128)(2,1)} fusion(f32[1728,1536]{1,0:T(8,128)} %fusion.26, f32[1728,1536]{1,0:T(8,128)} %fusion.29, f32[1728,1536]{1,0:T(8,128)} %fusion.31, f32[1728,1536]{1,0:T(8,128)} %fusion.33, f32[1728,1536]{1,0:T(8,128)} %fusion.35, f32[1728,1536]{1,0:T(8,128)} %fusion.37, f32[1728,1536]{1,0:T(8,128)} %fusion.41, ...), kind=kOutput, calls=%fused_computation.2 | convolution fusion | flops 1382842368 | bytes 91914240 | tf_op jit(solution)/shard_map/dot_general | solution.py:100
  245.2 149.6 %reduce-scatter.2.cloned.1.call-done = f32[48,9,256]{2,1,0:T(8,128)} async-done(((f32[1536,9,256]{2,1,0:T(8,128)}), f32[48,9,256]{2,1,0:T(8,128)}) %reduce-scatter.2.cloned.1.call-update) | async-done | bytes 442384 | tf_op jit(solution)/shard_map/reduce_scatter | solution.py:114
  (52 shorter events, 29.9 us)
Async XLA Ops:
  7.2 20.6 %copy-start = (f32[3,256]{1,0:T(4,128)S(1)}, f32[3,256]{1,0:T(4,128)}, u32[]{:S(2)}) copy-start(f32[3,256]{1,0:T(4,128)} %param.13) | copy-start | bytes 9220
  7.2 64.9 %copy-start.6 = (f32[256]{0:T(256)S(1)}, f32[256]{0:T(256)}, u32[]{:S(2)}) copy-start(f32[256]{0:T(256)} %param.11) | copy-start | bytes 3076
  7.2 64.9 %copy-start.7 = (f32[256]{0:T(256)S(1)}, f32[256]{0:T(256)}, u32[]{:S(2)}) copy-start(f32[256]{0:T(256)} %param.12) | copy-start | bytes 3076
  7.2 387.6 %reduce-scatter.2.cloned.1.call-start = ((), (), s32[]{:S(2)}) async-start(), calls=%async_computation.1 | async-start | bytes 25952256 | tf_op jit(solution)/shard_map/reduce_scatter | solution.py:114
  73.1 23.0 %slice-start = ((s8[5308416]{0:T(1024)(128)(4,1)}), s8[1114112]{0:T(1024)(128)(4,1)S(1)}, s32[]{:S(2)}) async-start(s8[5308416]{0:T(1024)(128)(4,1)} %bitcast.158), calls=%async_computation.2 | async-start | bytes 2228224
  84.5 11.5 %slice-start.1 = ((s8[5308416]{0:T(1024)(128)(4,1)}), s8[4194304]{0:T(1024)(128)(4,1)S(1)}, s32[]{:S(2)}) async-start(s8[5308416]{0:T(1024)(128)(4,1)} %bitcast.158), calls=%async_computation.3 | async-start | bytes 8388608
  86.9 3.5 collective-permute-start
  88.4 5.8 %collective-permute-start.1 = (bf16[2,12,72,256]{3,2,1,0:T(8,128)(2,1)S(1)}, bf16[2,12,72,256]{3,2,1,0:T(8,128)(2,1)S(1)}, u32[]{:S(2)}, u32[]{:S(2)}) collective-permute-start(bf16[2,12,72,256]{3,2,1,0:T(8,128)(2,1)S(1)} %bitcast.161), channel_id=1, source_target_pairs={{1,0},{2,1},{3,2},{5,4},{6,5},{7,6},{9,8},{10,9},{11,10},{13,12},{... | collective-permute-start | bytes 2654216 | tf_op jit(solution)/shard_map/ppermute | solution.py:20
  90.4 25.1 %copy-start.4 = (bf16[2,12,72,256]{3,2,1,0:T(8,128)(2,1)}, bf16[2,12,72,256]{3,2,1,0:T(8,128)(2,1)S(1)}, u32[]{:S(2)}) copy-start(bf16[2,12,72,256]{3,2,1,0:T(8,128)(2,1)S(1)} %collective-permute-done) | copy-start | bytes 2654212
  96.0 22.2 %copy-start.2 = (bf16[2,36,96,256]{3,2,1,0:T(8,128)(2,1)}, bf16[2,36,96,256]{3,2,1,0:T(8,128)(2,1)S(1)}, u32[]{:S(2)}) copy-start(bf16[2,36,96,256]{3,2,1,0:T(8,128)(2,1)S(1)} %fusion.5) | copy-start | bytes 10616836
  162.0 7.7 %copy-start.3 = (bf16[2,36,96,256]{3,2,1,0:T(8,128)(2,1)S(1)}, bf16[2,36,96,256]{3,2,1,0:T(8,128)(2,1)}, u32[]{:S(2)}) copy-start(bf16[2,36,96,256]{3,2,1,0:T(8,128)(2,1)} %copy-done.2) | copy-start | bytes 10616836
  169.7 8.8 %slice-start.2 = ((s8[7077888]{0:T(1024)(128)(4,1)}), s8[2883584]{0:T(1024)(128)(4,1)S(1)}, s32[]{:S(2)}) async-start(s8[7077888]{0:T(1024)(128)(4,1)} %bitcast.166), calls=%async_computation.4 | async-start | bytes 5767168
  170.3 8.2 %slice-start.3 = ((s8[7077888]{0:T(1024)(128)(4,1)}), s8[4194304]{0:T(1024)(128)(4,1)S(1)}, s32[]{:S(2)}) async-start(s8[7077888]{0:T(1024)(128)(4,1)} %bitcast.166), calls=%async_computation.5 | async-start | bytes 8388608
  208.9 6.2 %copy-start.5 = (bf16[2,12,72,256]{3,2,1,0:T(8,128)(2,1)S(1)}, bf16[2,12,72,256]{3,2,1,0:T(8,128)(2,1)}, u32[]{:S(2)}) copy-start(bf16[2,12,72,256]{3,2,1,0:T(8,128)(2,1)} %copy-done.4) | copy-start | bytes 2654212
  215.1 181.9 %copy-start.1 = (f32[3,256]{1,0:T(4,128)S(1)}, f32[3,256]{1,0:T(4,128)}, u32[]{:S(2)}) copy-start(f32[3,256]{1,0:T(4,128)} %param.13) | copy-start | bytes 9220
Sparse Core Ops, SparseCore 0:
  140.1 254.6 reduce-scatter.1
where the time goes:
time: 406 us; the launch traced here: 405 us
  waiting for transfers between devices  154 us (38%)
  matrix products  116 us (29%)
  blocking collectives  82.2 us (20%)
  local copies, waits for them, and re-layouts  22.6 us (6%)
  between operations  16.6 us (4%)
  other arithmetic  11.1 us (3%)
    reduce_scatter x1, waiting for transfers between devices, body(): lax.psum_scatter(jnp.stack(parts_list, 1), ('rep', 'tile'), scatter_dimen...  150 us
    dot_general x9, matrix products, body(): lax.dot_general(shifted_list[tap_index], conv_weight[tap_index], (((1,),...  82.6 us
    psum x1, blocking collectives, body(): lax.psum((jnp.sum(weights_pix), jnp.sum(weights_pix * cross)), ('rep', 't...  39.9 us
    dot_general x9, matrix products, body(): lax.dot_general(flat_x, shifted, (((0,), (0,)), ((), ())), preferred_elem...  25 us
    psum x1, blocking collectives, body(): lax.psum((first_gradient_sum, second_gradient_sum, class_tile), 'rep')  21.3 us
    another operation x1, local copies, waits for them, and re-layouts, body(): jnp.stack(parts_list, 1)  19 us
    psum x1, blocking collectives, body(): column_sum = lax.psum(jnp.sum(yvals, 0), 'tile')  8.36 us
  transfers between devices with their start and end apart: 3, of which 3 were waited for; matrix products, arithmetic and copies ran while one was open for 21% of the time, Pallas kernels for 0%

commit v1 on v0

--- a/solution.py
+++ b/solution.py
@@ -39,7 +39,7 @@
     per_replica_part = IMG_DEV * H * W
     all_pix = lax.axis_size("rep") * per_replica_part
     yvals = conv_out.astype(jnp.float32).reshape(local_pix, out_chans)
-    column_sum = lax.psum(jnp.sum(yvals, 0), "tile")
+    column_sum = jnp.sum(lax.all_gather(jnp.sum(yvals, 0), "tile"), axis=0)
     centre_offset = yvals - column_sum / per_replica_part
     variance = lax.psum(jnp.sum(centre_offset * centre_offset, 0), "tile") / per_replica_part
     inverse_deviation = lax.rsqrt(variance + 1e-05)

time: 406 us -> 405 us (level)
    psum x1 -> x0, blocking collectives: 8.36 us -> none  [body(): column_sum = lax.psum(jnp.sum(yvals, 0), 'tile')]
    all_gather x0 -> x1, blocking collectives: none -> 6 us  [body(): column_sum = jnp.sum(lax.all_gather(jnp.sum(yvals, 0), 'tile'), axis=0)]
where the time goes in v1:
time: 405 us; the launch traced here: 404 us
  waiting for transfers between devices  154 us (38%)
  matrix products  116 us (29%)
  blocking collectives  81.6 us (20%)
  local copies, waits for them, and re-layouts  22.6 us (6%)
  between operations  16.6 us (4%)
  other arithmetic  11.1 us (3%)
    reduce_scatter x1, waiting for transfers between devices, body(): lax.psum_scatter(jnp.stack(parts_list, 1), ('rep', 'tile'), scatter_dimen...  150 us
    dot_general x9, matrix products, body(): lax.dot_general(shifted_list[tap_index], conv_weight[tap_index], (((1,),...  82.6 us
    psum x1, blocking collectives, body(): lax.psum((jnp.sum(weights_pix), jnp.sum(weights_pix * cross)), ('rep', 't...  39.8 us
    dot_general x9, matrix products, body(): lax.dot_general(flat_x, shifted, (((0,), (0,)), ((), ())), preferred_elem...  25 us
    psum x1, blocking collectives, body(): lax.psum((first_gradient_sum, second_gradient_sum, class_tile), 'rep')  21.3 us
    another operation x1, local copies, waits for them, and re-layouts, body(): jnp.stack(parts_list, 1)  19 us
  transfers between devices with their start and end apart: 3, of which 3 were waited for; matrix products, arithmetic and copies ran while one was open for 21% of the time, Pallas kernels for 0%

profile of v1, /device:TPU:0, one launch (start us, length us, event | category | flops | bytes accessed | tf_op | source)
XLA Modules:
  0.0 404.4 jit_solution(14716452994521681616)
XLA Ops:
  8.7 6.0 %all-gather.1 = f32[4,1,256]{2,1,0:T(1,128)S(1)} all-gather(f32[1,1,256]{2,1,0:T(1,128)S(1)} %bitcast.176), channel_id=2, replica_groups=mesh['rep'=8,'tile'=4] {'tile'}, dimensions={0}, use_global_device_ids=true | all-gather | bytes 5120 | tf_op jit(solution)/shard_map/all_gather | solution.py:42
  16.2 7.6 %psum.63 = f32[256]{0:T(256)S(1)} all-reduce(f32[256]{0:T(256)S(1)} %multiply_reduce_fusion.1), channel_id=1, replica_groups=mesh['rep'=8,'tile'=4] {'tile'}, use_global_device_ids=true, to_apply=%region_3.0 | all-reduce | flops 256 | bytes 2048 | tf_op jit(solution)/shard_map/psum | solution.py:44
  31.0 39.8 %all-reduce.1 = (f32[]{:T(128)}, f32[]{:T(128)}) all-reduce(f32[]{:T(128)} %get-tuple-element.31, f32[]{:T(128)} %get-tuple-element.40), channel_id=1, replica_groups=mesh['rep'=8,'tile'=4] {'rep','tile'}, use_global_device_ids=true, to_apply=%region_6.0 | all-reduce | flops 2 | bytes 16 | tf_op jit(solution)/shard_map/psum | solution.py:57
  72.5 4.6 %fusion.61 = (f32[256]{0:T(256)S(1)}, f32[256]{0:T(256)S(1)}, f32[1728,256]{1,0:T(8,128)}) fusion(f32[256]{0:T(256)S(1)} %get-tuple-element.49, f32[256]{0:T(256)S(1)} %broadcast_multiply_fusion.1, bf16[2,12,72,256]{3,2,1,0:T(8,128)(2,1)} %param.9, f32[3,256]{1,0:T(4,128)S(1)} %copy-done, f32[1728,3]{0,1:T(4,128)S(1)} %get-tuple-element.51, ...), kind=kOutput, calls=%fused_computation.92 | convolution fusion | flops 20374336 | bytes 4474368 | tf_op jit(solution)/shard_map/dot_general | solution.py:65
  77.1 6.9 %all-reduce.3 = (f32[256]{0:T(256)S(1)}, f32[256]{0:T(256)S(1)}, f32[3,256]{1,0:T(4,128)S(1)}) all-reduce(f32[256]{0:T(256)S(1)} %get-tuple-element.25, f32[256]{0:T(256)S(1)} %get-tuple-element.24, f32[3,256]{1,0:T(4,128)S(1)} %fusion.16), channel_id=1, replica_groups=mesh['rep'=8,'tile'=4] {'tile'}, use_global_device_ids=true, to_apply=%region_12.13 | all-reduce | flops 1280 | bytes 10240 | tf_op jit(solution)/shard_map/psum | solution.py:67
  89.8 3.8 collective-permute-done.1
  95.5 2.8 fusion.14
  101.1 2.8 fusion.12
  103.9 2.8 fusion.11
  106.6 2.8 fusion.10
  109.4 2.8 fusion.9
  114.9 2.8 fusion.7
  120.5 19.0 %copy.18 = f32[1536,9,256]{2,1,0:T(8,128)} copy(f32[1536,9,256]{0,2,1:T(8,128)} %fusion.6) | data formatting | bytes 28311552 | tf_op jit(solution)/shard_map/stack | solution.py:115
  140.1 21.3 %all-reduce.2 = (f32[256]{0:T(256)}, f32[256]{0:T(256)}, f32[3,256]{1,0:T(4,128)}) all-reduce(f32[256]{0:T(256)S(1)} %get-tuple-element.37, f32[256]{0:T(256)S(1)} %get-tuple-element.38, f32[3,256]{1,0:T(4,128)S(1)} %get-tuple-element.39), channel_id=1, replica_groups=mesh['rep'=8,'tile'=4] {'rep'}, use_global_device_ids=true, to_apply=%region_14.15 | all-reduce | flops 1280 | bytes 10240 | tf_op jit(solution)/shard_map/psum | solution.py:75
  161.4 7.7 %fusion.33 = f32[1728,1536]{1,0:T(8,128)} fusion(bf16[1728,256]{1,0:T(8,128)(2,1)S(1)} %multiply_convert_fusion, bf16[9,1536,256]{2,1,0:T(8,128)(2,1)} %param.10), kind=kOutput, calls=%fused_computation.52 | convolution fusion | flops 1358954496 | bytes 12288000 | tf_op jit(solution)/shard_map/dot_general | solution.py:100
  169.8 8.2 %fusion.26 = f32[1728,1536]{1,0:T(8,128)} fusion(bf16[1728,256]{1,0:T(8,128)(2,1)S(1)} %bitcast.175, bf16[9,1536,256]{2,1,0:T(8,128)(2,1)} %param.10), kind=kOutput, calls=%fused_computation.45 | convolution fusion | flops 1358954496 | bytes 12288000 | tf_op jit(solution)/shard_map/dot_general | solution.py:100
  177.9 6.4 %fusion.29 = f32[1728,1536]{1,0:T(8,128)} fusion(bf16[1728,256]{1,0:T(8,128)(2,1)S(1)} %bitcast.174, bf16[9,1536,256]{2,1,0:T(8,128)(2,1)S(1)} %bitcast.168), kind=kOutput, calls=%fused_computation.48 | convolution fusion | flops 1358954496 | bytes 12288000 | tf_op jit(solution)/shard_map/dot_general | solution.py:100
  184.3 6.3 %fusion.31 = f32[1728,1536]{1,0:T(8,128)} fusion(bf16[1728,256]{1,0:T(8,128)(2,1)S(1)} %bitcast.173, bf16[9,1536,256]{2,1,0:T(8,128)(2,1)S(1)} %bitcast.168), kind=kOutput, calls=%fused_computation.50 | convolution fusion | flops 1358954496 | bytes 12288000 | tf_op jit(solution)/shard_map/dot_general | solution.py:100
  190.7 6.3 %fusion.35 = f32[1728,1536]{1,0:T(8,128)} fusion(bf16[1728,256]{1,0:T(8,128)(2,1)S(1)} %bitcast.172, bf16[9,1536,256]{2,1,0:T(8,128)(2,1)S(1)} %bitcast.168), kind=kOutput, calls=%fused_computation.54 | convolution fusion | flops 1358954496 | bytes 12288000 | tf_op jit(solution)/shard_map/dot_general | solution.py:100
  197.0 5.7 %fusion.37 = f32[1728,1536]{1,0:T(8,128)} fusion(bf16[1728,256]{1,0:T(8,128)(2,1)S(1)} %bitcast.171, bf16[9,1536,256]{2,1,0:T(8,128)(2,1)S(1)} %bitcast.168), kind=kOutput, calls=%fused_computation.56 | convolution fusion | flops 1358954496 | bytes 12288000 | tf_op jit(solution)/shard_map/dot_general | solution.py:100
  202.7 5.6 %fusion.41 = f32[1728,1536]{1,0:T(8,128)} fusion(bf16[1728,256]{1,0:T(8,128)(2,1)S(1)} %bitcast.170, bf16[9,1536,256]{2,1,0:T(8,128)(2,1)S(1)} %bitcast.168), kind=kOutput, calls=%fused_computation.60 | convolution fusion | flops 1358954496 | bytes 12288000 | tf_op jit(solution)/shard_map/dot_general | solution.py:100
  208.4 6.2 %fusion.39 = f32[1728,1536]{1,0:T(8,128)} fusion(bf16[1728,256]{1,0:T(8,128)(2,1)S(1)} %bitcast.165, bf16[9,1536,256]{2,1,0:T(8,128)(2,1)S(1)} %bitcast.168), kind=kOutput, calls=%fused_computation.58 | convolution fusion | flops 1358954496 | bytes 12288000 | tf_op jit(solution)/shard_map/dot_general | solution.py:100
  214.6 30.0 %add_convert_fusion = bf16[1728,1536]{1,0:T(8,128)(2,1)} fusion(f32[1728,1536]{1,0:T(8,128)} %fusion.26, f32[1728,1536]{1,0:T(8,128)} %fusion.29, f32[1728,1536]{1,0:T(8,128)} %fusion.31, f32[1728,1536]{1,0:T(8,128)} %fusion.33, f32[1728,1536]{1,0:T(8,128)} %fusion.35, f32[1728,1536]{1,0:T(8,128)} %fusion.37, f32[1728,1536]{1,0:T(8,128)} %fusion.41, ...), kind=kOutput, calls=%fused_computation.2 | convolution fusion | flops 1382842368 | bytes 91914240 | tf_op jit(solution)/shard_map/dot_general | solution.py:100
  244.6 149.6 %reduce-scatter.2.cloned.1.call-done = f32[48,9,256]{2,1,0:T(8,128)} async-done(((f32[1536,9,256]{2,1,0:T(8,128)}), f32[48,9,256]{2,1,0:T(8,128)}) %reduce-scatter.2.cloned.1.call-update) | async-done | bytes 442384 | tf_op jit(solution)/shard_map/reduce_scatter | solution.py:114
  (53 shorter events, 29.9 us)
Async XLA Ops:
  7.2 20.1 %copy-start = (f32[3,256]{1,0:T(4,128)S(1)}, f32[3,256]{1,0:T(4,128)}, u32[]{:S(2)}) copy-start(f32[3,256]{1,0:T(4,128)} %param.13) | copy-start | bytes 9220
  7.2 64.3 %copy-start.6 = (f32[256]{0:T(256)S(1)}, f32[256]{0:T(256)}, u32[]{:S(2)}) copy-start(f32[256]{0:T(256)} %param.11) | copy-start | bytes 3076
  7.2 64.3 %copy-start.7 = (f32[256]{0:T(256)S(1)}, f32[256]{0:T(256)}, u32[]{:S(2)}) copy-start(f32[256]{0:T(256)} %param.12) | copy-start | bytes 3076
  7.2 387.0 %reduce-scatter.2.cloned.1.call-start = ((), (), s32[]{:S(2)}) async-start(), calls=%async_computation.1 | async-start | bytes 25952256 | tf_op jit(solution)/shard_map/reduce_scatter | solution.py:114
  72.5 23.0 %slice-start = ((s8[5308416]{0:T(1024)(128)(4,1)}), s8[1114112]{0:T(1024)(128)(4,1)S(1)}, s32[]{:S(2)}) async-start(s8[5308416]{0:T(1024)(128)(4,1)} %bitcast.159), calls=%async_computation.2 | async-start | bytes 2228224
  83.9 11.5 %slice-start.1 = ((s8[5308416]{0:T(1024)(128)(4,1)}), s8[4194304]{0:T(1024)(128)(4,1)S(1)}, s32[]{:S(2)}) async-start(s8[5308416]{0:T(1024)(128)(4,1)} %bitcast.159), calls=%async_computation.3 | async-start | bytes 8388608
  86.3 3.5 collective-permute-start
  87.8 5.8 %collective-permute-start.1 = (bf16[2,12,72,256]{3,2,1,0:T(8,128)(2,1)S(1)}, bf16[2,12,72,256]{3,2,1,0:T(8,128)(2,1)S(1)}, u32[]{:S(2)}, u32[]{:S(2)}) collective-permute-start(bf16[2,12,72,256]{3,2,1,0:T(8,128)(2,1)S(1)} %bitcast.162), channel_id=1, source_target_pairs={{1,0},{2,1},{3,2},{5,4},{6,5},{7,6},{9,8},{10,9},{11,10},{13,12},{... | collective-permute-start | bytes 2654216 | tf_op jit(solution)/shard_map/ppermute | solution.py:20
  89.8 25.1 %copy-start.4 = (bf16[2,12,72,256]{3,2,1,0:T(8,128)(2,1)}, bf16[2,12,72,256]{3,2,1,0:T(8,128)(2,1)S(1)}, u32[]{:S(2)}) copy-start(bf16[2,12,72,256]{3,2,1,0:T(8,128)(2,1)S(1)} %collective-permute-done) | copy-start | bytes 2654212
  95.5 22.2 %copy-start.2 = (bf16[2,36,96,256]{3,2,1,0:T(8,128)(2,1)}, bf16[2,36,96,256]{3,2,1,0:T(8,128)(2,1)S(1)}, u32[]{:S(2)}) copy-start(bf16[2,36,96,256]{3,2,1,0:T(8,128)(2,1)S(1)} %fusion.5) | copy-start | bytes 10616836
  161.4 7.7 %copy-start.3 = (bf16[2,36,96,256]{3,2,1,0:T(8,128)(2,1)S(1)}, bf16[2,36,96,256]{3,2,1,0:T(8,128)(2,1)}, u32[]{:S(2)}) copy-start(bf16[2,36,96,256]{3,2,1,0:T(8,128)(2,1)} %copy-done.2) | copy-start | bytes 10616836
  169.1 8.8 %slice-start.2 = ((s8[7077888]{0:T(1024)(128)(4,1)}), s8[2883584]{0:T(1024)(128)(4,1)S(1)}, s32[]{:S(2)}) async-start(s8[7077888]{0:T(1024)(128)(4,1)} %bitcast.167), calls=%async_computation.4 | async-start | bytes 5767168
  169.7 8.2 %slice-start.3 = ((s8[7077888]{0:T(1024)(128)(4,1)}), s8[4194304]{0:T(1024)(128)(4,1)S(1)}, s32[]{:S(2)}) async-start(s8[7077888]{0:T(1024)(128)(4,1)} %bitcast.167), calls=%async_computation.5 | async-start | bytes 8388608
  208.4 6.2 %copy-start.5 = (bf16[2,12,72,256]{3,2,1,0:T(8,128)(2,1)S(1)}, bf16[2,12,72,256]{3,2,1,0:T(8,128)(2,1)}, u32[]{:S(2)}) copy-start(bf16[2,12,72,256]{3,2,1,0:T(8,128)(2,1)} %copy-done.4) | copy-start | bytes 2654212
  214.6 181.8 %copy-start.1 = (f32[3,256]{1,0:T(4,128)S(1)}, f32[3,256]{1,0:T(4,128)}, u32[]{:S(2)}) copy-start(f32[3,256]{1,0:T(4,128)} %param.13) | copy-start | bytes 9220
Sparse Core Ops, SparseCore 0:
  139.6 254.6 reduce-scatter.1
